TPU v7x, 512 devices: a whole 4x4x16 slice. The times are simulated.
512 devices in a mesh: head: 8 (over x, core), expert: 64 (over z, y).
Axes of the slice: x: 4, y: 4, z: 16, core: 2. Of those that a mesh axis runs over, the one named last changes fastest.
Arguments:
- q_latent: bfloat16 [512, 64, 512], P('expert', 'head'), may hold values from -16 to 16
- q_rotary: bfloat16 [512, 64, 64], P('expert', 'head'), may hold values from -3 to 3
- cache_latent: bfloat16 [512, 128, 512], P('expert'), may hold values from -5 to 5
- cache_rotary: bfloat16 [512, 64, 128], P('expert'), may hold values from -5 to 5
- lengths: int32 [512], P('expert'), may hold values from 16 to 128, as said below
- w_value_out: bfloat16 [32768, 5120], P('head', 'expert'), may hold values from -0.25 to 0.25
- resid: bfloat16 [512, 5120], P('expert'), may hold values from -8 to 8
- norm_gain: float32 [5120], replicated, may hold values from 0.1 to 1.9
- route_ids: int32 [512, 6], P('expert'), may hold values from 0 to 63, as said below
- route_weights: float32 [512, 6], P('expert'), may hold values from 0.1 to 0.6
- w_gate_up: bfloat16 [64, 2, 768, 5120], P('expert', None, 'head'), may hold values from -0.078125 to 0.078125
- w_down: bfloat16 [64, 768, 5120], P('expert', 'head'), may hold values from -0.21875 to 0.21875
Outputs:
- mixed_out: float32 [512, 5120], P('expert', 'head')
Inputs may be any that keep to these rules, and one draw needn't show every extreme that they name: `lengths`: slots at positions below a sequence's length are valid; some sequence has length 128. `route_ids`: each row names 6 different experts. Among the rows of one device (aligned blocks of 8 rows) no expert is named by more than 2 rows, and one expert is named by exactly 2 rows in every block.
All inputs are finite; a program needn't handle non-finite values.
Results may differ from a plain program's by a relative error of at most 0.0046.
Values may be sent and summed in bfloat16 or wider, within the bound.
No kernel may reach another device: no remote copies, remote signals or barrier semaphores. Data moves between devices by JAX's collectives and lax.ppermute only.
A program may use at most 64 MiB of HBM per device.

v0:
```python
import jax
import jax.numpy as jnp
from jax import lax
from jax.sharding import Mesh
from jax.sharding import PartitionSpec as P

EXPERT = ("ez", "ey")
softmax_scale = 192.0 ** (-0.5)
norm_epsilon = 1e-06


def attend(q_latent, q_rotary, cache_latent, cache_rotary, lengths):
    scores = jnp.einsum("shl,scl->shc", q_latent, cache_latent, preferred_element_type=jnp.float32)
    scores = scores + jnp.einsum(
        "shr,src->shc", q_rotary, cache_rotary, preferred_element_type=jnp.float32
    )
    scores = scores * softmax_scale
    position = lax.broadcasted_iota(jnp.int32, scores.shape, 2)
    scores = jnp.where(position < lengths[:, None, None], scores, -1e30)
    highest = jnp.max(scores, axis=2, keepdims=True)
    weights = jnp.exp(scores - highest)
    probs = (weights / jnp.sum(weights, axis=2, keepdims=True)).astype(jnp.bfloat16)
    return jnp.einsum(
        "shc,scl->shl", probs, cache_latent, preferred_element_type=jnp.float32
    ).astype(jnp.bfloat16)


def on_device(
    q_latent,
    q_rotary,
    cache_latent,
    cache_rotary,
    lengths,
    w_value_out,
    resid,
    norm_gain,
    route_ids,
    route_weights,
    w_gate_up,
    w_down,
):
    seq_local = q_latent.shape[0]
    latent_out = attend(q_latent, q_rotary, cache_latent, cache_rotary, lengths)
    flattened = latent_out.reshape(seq_local, -1)
    z_count = lax.axis_size("ez")
    latent_copies = jnp.broadcast_to(flattened[None], (z_count,) + flattened.shape)
    gathered = lax.all_to_all(latent_copies, "ez", split_axis=0, concat_axis=0, tiled=True)
    gathered = gathered.reshape(-1, flattened.shape[1])
    value_blocks = lax.all_gather(w_value_out, "ey", axis=0, tiled=False)
    column_terms = jnp.einsum(
        "sk,jkc->sjc", gathered, value_blocks, preferred_element_type=jnp.float32
    ).reshape(gathered.shape[0], -1)
    column_sums = lax.psum(column_terms, "head")
    attention = lax.all_to_all(
        column_sums.astype(jnp.bfloat16), "ez", split_axis=0, concat_axis=1, tiled=True
    )
    stream = resid.astype(jnp.float32) + attention.astype(jnp.float32)
    mean_square = jnp.mean(stream * stream, axis=1, keepdims=True)
    normed = (stream * lax.rsqrt(mean_square + norm_epsilon) * norm_gain).astype(jnp.bfloat16)
    expert_count = lax.axis_size("ez") * lax.axis_size("ey")
    top_count = route_ids.shape[1]
    capacity = max(2, -(-(seq_local * top_count) // expert_count))
    flat_ids = route_ids.reshape(-1)
    one_hot = (flat_ids[:, None] == jnp.arange(expert_count, dtype=jnp.int32)[None, :]).astype(
        jnp.int32
    )
    earlier = jnp.cumsum(one_hot, axis=0) - one_hot
    slot_index = jnp.sum(earlier * one_hot, axis=1)
    target = (flat_ids * capacity + slot_index).reshape(seq_local, top_count)
    places = jnp.arange(expert_count * capacity, dtype=jnp.int32)
    matches = target[None, :, :] == places[:, None, None]
    selector = jnp.sum(matches.astype(jnp.int32), axis=2).astype(jnp.bfloat16)
    blending = jnp.sum(jnp.where(matches, route_weights[None, :, :], 0.0), axis=2)
    gate_up = w_gate_up[0]
    col_width = stream.shape[1] // lax.axis_size("head")
    offset = lax.axis_index("head") * col_width
    normed_cols = lax.dynamic_slice_in_dim(normed, offset, col_width, 1)
    outgoing = jnp.dot(selector, normed_cols, preferred_element_type=jnp.float32).astype(
        jnp.bfloat16
    )
    outgoing = outgoing.reshape(expert_count, capacity, -1)
    arrived = lax.all_to_all(outgoing, EXPERT, split_axis=0, concat_axis=0, tiled=True)
    arrived_cols = arrived.reshape(-1, arrived.shape[2])
    head_count = lax.axis_size("head")
    down_blocks = w_down[0].reshape(w_down.shape[1], head_count, -1)
    arrived_cols, down_blocks = lax.optimization_barrier((arrived_cols, down_blocks))
    down_cols = lax.all_to_all(down_blocks, "head", split_axis=1, concat_axis=0, tiled=True)
    down_cols = down_cols.reshape(-1, down_blocks.shape[2])
    flat_rows = lax.all_gather(arrived_cols, "head", axis=1, tiled=True)
    projected = jnp.einsum("rd,gfd->rgf", flat_rows, gate_up, preferred_element_type=jnp.float32)
    hidden = (jax.nn.silu(projected[:, 0]) * projected[:, 1]).astype(jnp.bfloat16)
    hidden_all = lax.all_gather(hidden, "head", axis=1, tiled=True)
    summed_cols = jnp.dot(hidden_all, down_cols, preferred_element_type=jnp.float32).astype(
        jnp.bfloat16
    )
    summed_rows = summed_cols.reshape(expert_count, capacity, -1)
    returned = lax.all_to_all(summed_rows, EXPERT, split_axis=0, concat_axis=0, tiled=True)
    back_rows = returned.reshape(expert_count * capacity, -1).astype(jnp.float32)
    mixture = jnp.dot(blending.T, back_rows, precision=lax.Precision.HIGHEST)
    stream_cols = lax.dynamic_slice_in_dim(stream, offset, col_width, 1)
    return stream_cols + mixture


def solution(mesh):
    placed = (
        P(EXPERT, "head", None),
        P(EXPERT, "head", None),
        P(EXPERT, None, None),
        P(EXPERT, None, None),
        P(EXPERT),
        P("head", EXPERT),
        P(EXPERT, None),
        P(),
        P(EXPERT, None),
        P(EXPERT, None),
        P(EXPERT, None, "head", None),
        P(EXPERT, "head", None),
    )
    head_count, expert_total = mesh.devices.shape
    y_count = len({device.coords[1] for device in mesh.devices[0]})
    split_mesh = Mesh(
        mesh.devices.reshape(head_count, expert_total // y_count, y_count), ("head",) + EXPERT
    )
    return jax.shard_map(
        on_device, mesh=split_mesh, in_specs=placed, out_specs=P(EXPERT, "head"), check_vma=False
    )
```

profile of v0, /device:TPU:8, one launch (start us, length us, event | category | flops | bytes accessed | tf_op | source)
XLA Modules:
  0.0 234.2 jit_solution(10736050746131402408)
XLA Ops:
  6.5 0.7 all-gather.6.cloned.1.call-update
  7.3 1.6 fusion.20
  8.9 1.1 fusion.8
  10.1 0.3 fusion.4
  10.5 1.1 broadcast_in_dim.33
  11.6 15.2 %all-to-all-start = ((bf16[16,8,4096]{2,1,0:T(8,128)(2,1)}), bf16[16,8,4096]{2,1,0:T(8,128)(2,1)S(1)}, u32[]{:S(2)}, u32[]{:S(2)}) async-start(bf16[16,8,4096]{2,1,0:T(8,128)(2,1)} %broadcast_in_dim.33), calls=%async_computation | async-start | bytes 2097152 | tf_op jit(solution)/shard_map/all_to_all | solution.py:47
  27.3 28.6 %all-gather.6.cloned.1.call-done = bf16[16384,80]{0,1:T(8,128)(2,1)} async-done(((bf16[4096,80]{0,1:T(8,128)(2,1)}), bf16[16384,80]{0,1:T(8,128)(2,1)}) %all-gather.6.cloned.1.call-update) | async-done | bytes 2621456 | tf_op jit(solution)/shard_map/all_gather | solution.py:49
  55.9 5.5 %reshape.55 = bf16[4,4096,80]{1,0,2:T(4,128)(2,1)} reshape(bf16[16384,80]{0,1:T(8,128)(2,1)} %all-gather.6.cloned.1.call-done) | data formatting | bytes 5242880 | tf_op jit(solution)/shard_map/all_gather | solution.py:49
  61.4 4.7 %copy.24 = bf16[4,80,4096]{2,1,0:T(8,128)(2,1)} copy(bf16[4,80,4096]{2,0,1:T(4,128)(2,1)} %bitcast.50) | data formatting | bytes 5242880 | tf_op jit(solution)/shard_map/sk,jkc->sjc/dot_general | solution.py:50
  66.1 10.7 %all-to-all-done = bf16[16,8,4096]{2,1,0:T(8,128)(2,1)S(1)} async-done(((bf16[16,8,4096]{2,1,0:T(8,128)(2,1)}), bf16[16,8,4096]{2,1,0:T(8,128)(2,1)S(1)}, u32[]{:S(2)}, u32[]{:S(2)}) %all-to-all-start) | async-done | bytes 1048608 | tf_op jit(solution)/shard_map/all_to_all | solution.py:47
  76.8 2.6 %fusion.9 = f32[128,320]{0,1:T(8,128)S(1)} fusion(bf16[320,4096]{1,0:T(8,128)(2,1)} %bitcast.49, bf16[16,8,4096]{2,1,0:T(8,128)(2,1)S(1)} %all-to-all-done), kind=kOutput, calls=%fused_computation.14 | convolution fusion | flops 335544320 | bytes 3833856 | tf_op jit(solution)/shard_map/sk,jkc->sjc/dot_general | solution.py:50
  79.4 25.1 %all-reduce.1 = bf16[128,320]{0,1:T(8,128)(2,1)S(1)} all-reduce(f32[128,320]{0,1:T(8,128)S(1)} %fusion.9), channel_id=1, replica_groups=mesh['head'=8,'ez'=16,'ey'=4] {'head'}, use_global_device_ids=true, to_apply=%region_2.3 | all-reduce | flops 40960 | bytes 245760 | tf_op jit(solution)/shard_map/psum | solution.py:53
  104.5 0.7 copy.25
  105.2 10.2 %all-to-all-start.1 = ((bf16[16,8,320]{2,1,0:T(8,128)(2,1)}), bf16[16,8,320]{2,1,0:T(8,128)(2,1)S(1)}, u32[]{:S(2)}, u32[]{:S(2)}) async-start(bf16[16,8,320]{2,1,0:T(8,128)(2,1)} %bitcast.3), calls=%async_computation.1 | async-start | bytes 196608 | tf_op jit(solution)/shard_map/all_to_all | solution.py:54
  115.6 0.8 dynamic-slice
  116.4 12.1 %all-to-all-done.1 = bf16[16,8,320]{2,1,0:T(8,128)(2,1)S(1)} async-done(((bf16[16,8,320]{2,1,0:T(8,128)(2,1)}), bf16[16,8,320]{2,1,0:T(8,128)(2,1)S(1)}, u32[]{:S(2)}, u32[]{:S(2)}) %all-to-all-start.1) | async-done | bytes 81952 | tf_op jit(solution)/shard_map/all_to_all | solution.py:54
  128.8 0.3 convolution_convert_fusion.1
  129.1 0.7 reshape.49
  129.9 7.0 %all-to-all-start.2 = ((bf16[64,2,640]{2,1,0:T(2,128)(2,1)}), bf16[64,2,640]{2,1,0:T(2,128)(2,1)S(1)}, u32[]{:S(2)}, u32[]{:S(2)}) async-start(bf16[64,2,640]{2,1,0:T(2,128)(2,1)} %reshape.49), calls=%async_computation.2 | async-start | bytes 327680 | tf_op jit(solution)/shard_map/all_to_all | solution.py:82
  136.9 1.3 copy.31
  138.2 14.4 %all-to-all-done.2 = bf16[64,2,640]{2,1,0:T(2,128)(2,1)S(1)} async-done(((bf16[64,2,640]{2,1,0:T(2,128)(2,1)}), bf16[64,2,640]{2,1,0:T(2,128)(2,1)S(1)}, u32[]{:S(2)}, u32[]{:S(2)}) %all-to-all-start.2) | async-done | bytes 163872 | tf_op jit(solution)/shard_map/all_to_all | solution.py:82
  152.6 0.7 reshape.50
  153.3 1.1 copy.29
  154.4 5.0 %all-to-all-start.3 = ((bf16[96,8,640]{2,0,1:T(8,128)(2,1)}), bf16[96,8,640]{2,0,1:T(8,128)(2,1)S(1)}, u32[]{:S(2)}, u32[]{:S(2)}) async-start(bf16[96,8,640]{2,0,1:T(8,128)(2,1)} %copy.29), calls=%async_computation.3 | async-start | bytes 1966080 | tf_op jit(solution)/shard_map/all_to_all | solution.py:87
  159.4 19.3 %all-gather.4.cloned.1.call-done = bf16[128,5120]{1,0:T(8,128)(2,1)} async-done(((bf16[128,640]{1,0:T(8,128)(2,1)}), bf16[128,5120]{1,0:T(8,128)(2,1)}) %all-gather.4.cloned.1.call-update) | async-done | bytes 1310736 | tf_op jit(solution)/shard_map/all_gather | solution.py:89
  178.7 2.0 fusion.1
  180.8 12.8 %all_gather.15 = bf16[128,768]{0,1:T(8,128)(2,1)S(1)} all-gather(bf16[128,96]{0,1:T(8,128)(2,1)S(1)} %fusion.12), channel_id=1, replica_groups=mesh['head'=8,'ez'=16,'ey'=4] {'head'}, dimensions={1}, use_global_device_ids=true | all-gather | bytes 221184 | tf_op jit(solution)/shard_map/all_gather | solution.py:92
  193.6 0.3 convolution_convert_fusion
  193.9 0.7 reshape.52
  194.6 13.5 %all-to-all-start.4 = ((bf16[64,2,640]{2,1,0:T(2,128)(2,1)}), bf16[64,2,640]{2,1,0:T(2,128)(2,1)S(1)}, u32[]{:S(2)}, u32[]{:S(2)}) async-start(bf16[64,2,640]{2,1,0:T(2,128)(2,1)} %reshape.52), calls=%async_computation.4 | async-start | bytes 327680 | tf_op jit(solution)/shard_map/all_to_all | solution.py:97
  208.3 18.2 %all-to-all-done.4 = bf16[64,2,640]{2,1,0:T(2,128)(2,1)S(1)} async-done(((bf16[64,2,640]{2,1,0:T(2,128)(2,1)}), bf16[64,2,640]{2,1,0:T(2,128)(2,1)S(1)}, u32[]{:S(2)}, u32[]{:S(2)}) %all-to-all-start.4) | async-done | bytes 163872 | tf_op jit(solution)/shard_map/all_to_all | solution.py:97
  226.6 0.8 convolution_add_fusion.1
  (33 shorter events, 1.5 us)
Async XLA Ops:
  6.5 172.2 %copy-start = (bf16[1,2,96,5120]{3,2,1,0:T(8,128)(2,1)S(1)}, bf16[1,2,96,5120]{3,2,1,0:T(8,128)(2,1)}, u32[]{:S(2)}) copy-start(bf16[1,2,96,5120]{3,2,1,0:T(8,128)(2,1)} %param.22) | copy-start | bytes 5898244
  6.5 3.6 %copy-start.1 = (bf16[8,128,512]{2,1,0:T(8,128)(2,1)S(1)}, bf16[8,128,512]{2,1,0:T(8,128)(2,1)}, u32[]{:S(2)}) copy-start(bf16[8,128,512]{2,1,0:T(8,128)(2,1)} %param.14) | copy-start | bytes 3145732
  6.5 49.3 %all-gather.6.cloned.1.call-start = ((), (), s32[]{:S(2)}) async-start(), calls=%async_computation.6 | async-start | bytes 3276800 | tf_op jit(solution)/shard_map/all_gather | solution.py:49
  10.4 16.4 %copy-start.3 = (s32[8,6]{1,0:T(8,128)S(1)}, s32[8,6]{1,0:T(8,128)}, u32[]{:S(2)}) copy-start(s32[8,6]{1,0:T(8,128)} %param.20) | copy-start | bytes 580
  11.6 65.2 %all-to-all-start = ((bf16[16,8,4096]{2,1,0:T(8,128)(2,1)}), bf16[16,8,4096]{2,1,0:T(8,128)(2,1)S(1)}, u32[]{:S(2)}, u32[]{:S(2)}) async-start(bf16[16,8,4096]{2,1,0:T(8,128)(2,1)} %broadcast_in_dim.33), calls=%async_computation | async-start | bytes 2097152 | tf_op jit(solution)/shard_map/all_to_all | solution.py:47
  76.8 51.9 %copy-start.2 = (bf16[8,5120]{1,0:T(8,128)(2,1)S(1)}, bf16[8,5120]{1,0:T(8,128)(2,1)}, u32[]{:S(2)}) copy-start(bf16[8,5120]{1,0:T(8,128)(2,1)} %param.18) | copy-start | bytes 245764
  105.2 23.2 %all-to-all-start.1 = ((bf16[16,8,320]{2,1,0:T(8,128)(2,1)}), bf16[16,8,320]{2,1,0:T(8,128)(2,1)S(1)}, u32[]{:S(2)}, u32[]{:S(2)}) async-start(bf16[16,8,320]{2,1,0:T(8,128)(2,1)} %bitcast.3), calls=%async_computation.1 | async-start | bytes 196608 | tf_op jit(solution)/shard_map/all_to_all | solution.py:54
  129.9 22.7 %all-to-all-start.2 = ((bf16[64,2,640]{2,1,0:T(2,128)(2,1)}), bf16[64,2,640]{2,1,0:T(2,128)(2,1)S(1)}, u32[]{:S(2)}, u32[]{:S(2)}) async-start(bf16[64,2,640]{2,1,0:T(2,128)(2,1)} %reshape.49), calls=%async_computation.2 | async-start | bytes 327680 | tf_op jit(solution)/shard_map/all_to_all | solution.py:82
  136.8 41.9 %all-gather.4.cloned.1.call-start = ((), (), s32[]{:S(2)}) async-start(), calls=%async_computation.5 | async-start | bytes 1474560 | tf_op jit(solution)/shard_map/all_gather | solution.py:89
  154.4 39.1 %all-to-all-start.3 = ((bf16[96,8,640]{2,0,1:T(8,128)(2,1)}), bf16[96,8,640]{2,0,1:T(8,128)(2,1)S(1)}, u32[]{:S(2)}, u32[]{:S(2)}) async-start(bf16[96,8,640]{2,0,1:T(8,128)(2,1)} %copy.29), calls=%async_computation.3 | async-start | bytes 1966080 | tf_op jit(solution)/shard_map/all_to_all | solution.py:87
  180.7 27.4 %copy-start.4 = (f32[8,6]{1,0:T(8,128)S(1)}, f32[8,6]{1,0:T(8,128)}, u32[]{:S(2)}) copy-start(f32[8,6]{1,0:T(8,128)} %param.21) | copy-start | bytes 580
  194.6 31.9 %all-to-all-start.4 = ((bf16[64,2,640]{2,1,0:T(2,128)(2,1)}), bf16[64,2,640]{2,1,0:T(2,128)(2,1)S(1)}, u32[]{:S(2)}, u32[]{:S(2)}) async-start(bf16[64,2,640]{2,1,0:T(2,128)(2,1)} %reshape.52), calls=%async_computation.4 | async-start | bytes 327680 | tf_op jit(solution)/shard_map/all_to_all | solution.py:97
Sparse Core Ops, SparseCore 0:
  9.5 46.3 all-gather.5
  153.5 25.2 all-gather.3
where the time goes:
time: 235 us; the launch traced here: 234 us
  waiting for transfers between devices  104 us (44%)
  starting transfers between devices  50.9 us (22%)
  blocking collectives  37.9 us (16%)
  local copies, waits for them, and re-layouts  18 us (8%)
  between operations  13.6 us (6%)
  matrix products  9.05 us (4%)
    all_gather x1, waiting for transfers between devices, on_device(): value_blocks = lax.all_gather(w_value_out, 'ey', axis=0, tiled=False)  28.6 us
    psum x1, blocking collectives, on_device(): column_sums = lax.psum(column_terms, 'head')  25.1 us
    all_gather x1, waiting for transfers between devices, on_device(): flat_rows = lax.all_gather(arrived_cols, 'head', axis=1, tiled=True)  19.3 us
    all_to_all x1, waiting for transfers between devices, on_device(): lax.all_to_all(summed_rows, EXPERT, split_axis=0, concat_axis=0, tiled=True)  18.2 us
    all_to_all x1, starting transfers between devices, on_device(): lax.all_to_all(latent_copies, 'ez', split_axis=0, concat_axis=0, tiled=True)  15.2 us
    all_to_all x1, waiting for transfers between devices, on_device(): lax.all_to_all(outgoing, EXPERT, split_axis=0, concat_axis=0, tiled=True)  14.4 us
    all_to_all x1, starting transfers between devices, on_device(): lax.all_to_all(summed_rows, EXPERT, split_axis=0, concat_axis=0, tiled=True)  13.5 us
    all_gather x1, blocking collectives, on_device(): hidden_all = lax.all_gather(hidden, 'head', axis=1, tiled=True)  12.8 us
  transfers between devices with their start and end apart: 7, of which 6 were waited for; matrix products, arithmetic and copies ran while one was open for 9% of the time, Pallas kernels for 0%

commit v1 on v0

--- a/solution.py
+++ b/solution.py
@@ -86,7 +86,23 @@
     arrived_cols, down_blocks = lax.optimization_barrier((arrived_cols, down_blocks))
     down_cols = lax.all_to_all(down_blocks, "head", split_axis=1, concat_axis=0, tiled=True)
     down_cols = down_cols.reshape(-1, down_blocks.shape[2])
-    flat_rows = lax.all_gather(arrived_cols, "head", axis=1, tiled=True)
+
+    def make_the_blocks(frame, mesh_name):
+        degree = jax.lax.psum(1, mesh_name)
+        pile = [(src_i, (src_i + 1) % degree) for src_i in range(degree)]
+        heap = [(src_i, (src_i - 1) % degree) for src_i in range(degree)]
+        inter, tmp = ([frame], [frame])
+        for _ in range(degree // 2):
+            odd = jax.lax.ppermute(inter[-1], mesh_name, pile)
+            inter.append(odd)
+        for _ in tuple(range((degree - 1) // 2)):
+            t_next = jax.lax.ppermute(tmp[-1], mesh_name, heap)
+            tmp.append(t_next)
+        e_now = jnp.concatenate([*inter[::-1], *tmp[1:]], 1)
+        far_arr = jax.lax.axis_index(mesh_name)
+        return jnp.roll(e_now, (far_arr - degree // 2) * frame.shape[1], 1)
+
+    flat_rows = make_the_blocks(arrived_cols, "head")
     projected = jnp.einsum("rd,gfd->rgf", flat_rows, gate_up, preferred_element_type=jnp.float32)
     hidden = (jax.nn.silu(projected[:, 0]) * projected[:, 1]).astype(jnp.bfloat16)
     hidden_all = lax.all_gather(hidden, "head", axis=1, tiled=True)

time: 235 us -> 244 us (1.038)
  the two profiles are of different devices: /device:TPU:8 before, /device:TPU:2 now
where the time goes in v1:
time: 244 us; the launch traced here: 243 us
  waiting for transfers between devices  107 us (44%)
  starting transfers between devices  52.1 us (21%)
  blocking collectives  34.8 us (14%)
  local copies, waits for them, and re-layouts  24.8 us (10%)
  between operations  13.7 us (6%)
  matrix products  9.82 us (4%)
    all_gather x1, waiting for transfers between devices, on_device(): value_blocks = lax.all_gather(w_value_out, 'ey', axis=0, tiled=False)  28.3 us
    psum x1, blocking collectives, on_device(): column_sums = lax.psum(column_terms, 'head')  22 us
    all_to_all x1, waiting for transfers between devices, on_device(): lax.all_to_all(summed_rows, EXPERT, split_axis=0, concat_axis=0, tiled=True)  19.6 us
    all_to_all x1, waiting for transfers between devices, on_device(): lax.all_to_all(outgoing, EXPERT, split_axis=0, concat_axis=0, tiled=True)  15.4 us
    all_to_all x1, starting transfers between devices, on_device(): lax.all_to_all(latent_copies, 'ez', split_axis=0, concat_axis=0, tiled=True)  15.2 us
    all_gather x1, blocking collectives, on_device(): hidden_all = lax.all_gather(hidden, 'head', axis=1, tiled=True)  12.8 us
    all_to_all x1, waiting for transfers between devices, on_device(): lax.all_to_all(column_sums.astype(jnp.bfloat16), 'ez', split_axis=0, conc...  12.1 us
    all_to_all x1, starting transfers between devices, on_device(): lax.all_to_all(down_blocks, 'head', split_axis=1, concat_axis=0, tiled=True)  11 us
  transfers between devices with their start and end apart: 13, of which 9 were waited for; matrix products, arithmetic and copies ran while one was open for 11% of the time, Pallas kernels for 0%

profile of v1, /device:TPU:2, one launch (start us, length us, event | category | flops | bytes accessed | tf_op | source)
XLA Modules:
  0.0 243.2 jit_solution(5605383662681984592)
XLA Ops:
  7.3 1.6 fusion.22
  8.9 1.1 fusion.9
  10.1 1.5 fusion.5
  11.7 1.1 broadcast_in_dim.33
  12.8 15.2 %all-to-all-start = ((bf16[16,8,4096]{2,1,0:T(8,128)(2,1)}), bf16[16,8,4096]{2,1,0:T(8,128)(2,1)S(1)}, u32[]{:S(2)}, u32[]{:S(2)}) async-start(bf16[16,8,4096]{2,1,0:T(8,128)(2,1)} %broadcast_in_dim.33), calls=%async_computation | async-start | bytes 2097152 | tf_op jit(solution)/shard_map/all_to_all | solution.py:47
  28.5 28.3 %all-gather.3.cloned.1.call-done = bf16[16384,80]{0,1:T(8,128)(2,1)} async-done(((bf16[4096,80]{0,1:T(8,128)(2,1)}), bf16[16384,80]{0,1:T(8,128)(2,1)}) %all-gather.3.cloned.1.call-update) | async-done | bytes 2621456 | tf_op jit(solution)/shard_map/all_gather | solution.py:49
  56.8 5.5 %reshape.55 = bf16[4,4096,80]{1,0,2:T(4,128)(2,1)} reshape(bf16[16384,80]{0,1:T(8,128)(2,1)} %all-gather.3.cloned.1.call-done) | data formatting | bytes 5242880 | tf_op jit(solution)/shard_map/all_gather | solution.py:49
  62.4 4.7 %copy.24 = bf16[4,80,4096]{2,1,0:T(8,128)(2,1)} copy(bf16[4,80,4096]{2,0,1:T(4,128)(2,1)} %bitcast.50) | data formatting | bytes 5242880 | tf_op jit(solution)/shard_map/sk,jkc->sjc/dot_general | solution.py:50
  67.0 11.0 %all-to-all-done = bf16[16,8,4096]{2,1,0:T(8,128)(2,1)S(1)} async-done(((bf16[16,8,4096]{2,1,0:T(8,128)(2,1)}), bf16[16,8,4096]{2,1,0:T(8,128)(2,1)S(1)}, u32[]{:S(2)}, u32[]{:S(2)}) %all-to-all-start) | async-done | bytes 1048608 | tf_op jit(solution)/shard_map/all_to_all | solution.py:47
  78.0 2.6 %fusion.10 = f32[128,320]{0,1:T(8,128)S(1)} fusion(bf16[320,4096]{1,0:T(8,128)(2,1)} %bitcast.49, bf16[16,8,4096]{2,1,0:T(8,128)(2,1)S(1)} %all-to-all-done), kind=kOutput, calls=%fused_computation.15 | convolution fusion | flops 335544320 | bytes 3833856 | tf_op jit(solution)/shard_map/sk,jkc->sjc/dot_general | solution.py:50
  80.6 22.0 %all-reduce.1 = bf16[128,320]{0,1:T(8,128)(2,1)S(1)} all-reduce(f32[128,320]{0,1:T(8,128)S(1)} %fusion.10), channel_id=1, replica_groups=mesh['head'=8,'ez'=16,'ey'=4] {'head'}, use_global_device_ids=true, to_apply=%region_2.3 | all-reduce | flops 40960 | bytes 245760 | tf_op jit(solution)/shard_map/psum | solution.py:53
  103.4 10.2 %all-to-all-start.1 = ((bf16[16,8,320]{2,1,0:T(8,128)(2,1)}), bf16[16,8,320]{2,1,0:T(8,128)(2,1)S(1)}, u32[]{:S(2)}, u32[]{:S(2)}) async-start(bf16[16,8,320]{2,1,0:T(8,128)(2,1)} %bitcast.3), calls=%async_computation.1 | async-start | bytes 196608 | tf_op jit(solution)/shard_map/all_to_all | solution.py:54
  114.6 12.1 %all-to-all-done.1 = bf16[16,8,320]{2,1,0:T(8,128)(2,1)S(1)} async-done(((bf16[16,8,320]{2,1,0:T(8,128)(2,1)}), bf16[16,8,320]{2,1,0:T(8,128)(2,1)S(1)}, u32[]{:S(2)}, u32[]{:S(2)}) %all-to-all-start.1) | async-done | bytes 81952 | tf_op jit(solution)/shard_map/all_to_all | solution.py:54
  128.6 7.0 %all-to-all-start.2 = ((bf16[64,2,640]{2,1,0:T(2,128)(2,1)}), bf16[64,2,640]{2,1,0:T(2,128)(2,1)S(1)}, u32[]{:S(2)}, u32[]{:S(2)}) async-start(bf16[64,2,640]{2,1,0:T(2,128)(2,1)} %reshape.49), calls=%async_computation.2 | async-start | bytes 327680 | tf_op jit(solution)/shard_map/all_to_all | solution.py:82
  135.6 1.3 copy.31
  137.0 15.4 %all-to-all-done.2 = bf16[64,2,640]{2,1,0:T(2,128)(2,1)S(1)} async-done(((bf16[64,2,640]{2,1,0:T(2,128)(2,1)}), bf16[64,2,640]{2,1,0:T(2,128)(2,1)S(1)}, u32[]{:S(2)}, u32[]{:S(2)}) %all-to-all-start.2) | async-done | bytes 163872 | tf_op jit(solution)/shard_map/all_to_all | solution.py:82
  152.5 4.7 %collective-permute-done = bf16[128,640]{1,0:T(8,128)(2,1)S(1)} collective-permute-done((bf16[128,640]{1,0:T(8,128)(2,1)S(1)}, bf16[128,640]{1,0:T(8,128)(2,1)S(1)}, u32[]{:S(2)}, u32[]{:S(2)}) %collective-permute-start) | collective-permute-done | bytes 163872 | tf_op jit(solution)/shard_map/ppermute | solution.py:96
  157.8 1.1 collective-permute-start.4
  159.0 3.0 %collective-permute-done.1 = bf16[128,640]{1,0:T(8,128)(2,1)S(1)} collective-permute-done((bf16[128,640]{1,0:T(8,128)(2,1)S(1)}, bf16[128,640]{1,0:T(8,128)(2,1)S(1)}, u32[]{:S(2)}, u32[]{:S(2)}) %collective-permute-start.1) | collective-permute-done | bytes 163872 | tf_op jit(solution)/shard_map/ppermute | solution.py:96
  162.7 1.1 collective-permute-start.5
  163.8 3.1 %collective-permute-done.2 = bf16[128,640]{1,0:T(8,128)(2,1)} collective-permute-done((bf16[128,640]{1,0:T(8,128)(2,1)S(1)}, bf16[128,640]{1,0:T(8,128)(2,1)}, u32[]{:S(2)}, u32[]{:S(2)}) %collective-permute-start.2) | collective-permute-done | bytes 163872 | tf_op jit(solution)/shard_map/ppermute | solution.py:96
  167.3 1.1 copy.29
  168.4 11.0 %all-to-all-start.3 = ((bf16[96,8,640]{2,0,1:T(8,128)(2,1)}), bf16[96,8,640]{2,0,1:T(8,128)(2,1)S(1)}, u32[]{:S(2)}, u32[]{:S(2)}) async-start(bf16[96,8,640]{2,0,1:T(8,128)(2,1)} %copy.29), calls=%async_computation.3 | async-start | bytes 1966080 | tf_op jit(solution)/shard_map/all_to_all | solution.py:87
  182.5 0.9 constant_dynamic-update-slice_fusion.9
  183.4 9.2 %collective-permute-done.6 = bf16[128,640]{1,0:T(8,128)(2,1)S(1)} collective-permute-done((bf16[128,640]{1,0:T(8,128)(2,1)}, bf16[128,640]{1,0:T(8,128)(2,1)S(1)}, u32[]{:S(2)}, u32[]{:S(2)}) %collective-permute-start.6) | collective-permute-done | bytes 163872 | tf_op jit(solution)/shard_map/ppermute | solution.py:99
  192.6 0.9 constant_dynamic-update-slice_fusion.7
  193.6 0.9 constant_dynamic-update-slice_fusion.6
  194.6 0.9 constant_dynamic-update-slice_fusion.1
  196.5 12.8 %all_gather.11 = bf16[128,768]{0,1:T(8,128)(2,1)S(1)} all-gather(bf16[128,96]{0,1:T(8,128)(2,1)S(1)} %fusion.13), channel_id=1, replica_groups=mesh['head'=8,'ez'=16,'ey'=4] {'head'}, dimensions={1}, use_global_device_ids=true | all-gather | bytes 221184 | tf_op jit(solution)/shard_map/all_gather | solution.py:108
  210.3 4.6 %all-to-all-start.4 = ((bf16[64,2,640]{2,1,0:T(2,128)(2,1)}), bf16[64,2,640]{2,1,0:T(2,128)(2,1)S(1)}, u32[]{:S(2)}, u32[]{:S(2)}) async-start(bf16[64,2,640]{2,1,0:T(2,128)(2,1)} %reshape.52), calls=%async_computation.4 | async-start | bytes 327680 | tf_op jit(solution)/shard_map/all_to_all | solution.py:113
  215.1 19.6 %all-to-all-done.4 = bf16[64,2,640]{2,1,0:T(2,128)(2,1)S(1)} async-done(((bf16[64,2,640]{2,1,0:T(2,128)(2,1)}), bf16[64,2,640]{2,1,0:T(2,128)(2,1)S(1)}, u32[]{:S(2)}, u32[]{:S(2)}) %all-to-all-start.4) | async-done | bytes 163872 | tf_op jit(solution)/shard_map/all_to_all | solution.py:113
  234.8 1.5 convolution_add_fusion.1
  (64 shorter events, 12.2 us)
Async XLA Ops:
  6.5 189.1 %copy-start = (bf16[1,2,96,5120]{3,2,1,0:T(8,128)(2,1)S(1)}, bf16[1,2,96,5120]{3,2,1,0:T(8,128)(2,1)}, u32[]{:S(2)}) copy-start(bf16[1,2,96,5120]{3,2,1,0:T(8,128)(2,1)} %param.22) | copy-start | bytes 5898244
  6.5 50.3 %all-gather.3.cloned.1.call-start = ((), (), s32[]{:S(2)}) async-start(), calls=%async_computation.5 | async-start | bytes 3276800 | tf_op jit(solution)/shard_map/all_gather | solution.py:49
  8.9 19.2 %copy-start.5 = (s32[8,6]{1,0:T(8,128)S(1)}, s32[8,6]{1,0:T(8,128)}, u32[]{:S(2)}) copy-start(s32[8,6]{1,0:T(8,128)} %param.20) | copy-start | bytes 580
  12.8 65.2 %all-to-all-start = ((bf16[16,8,4096]{2,1,0:T(8,128)(2,1)}), bf16[16,8,4096]{2,1,0:T(8,128)(2,1)S(1)}, u32[]{:S(2)}, u32[]{:S(2)}) async-start(bf16[16,8,4096]{2,1,0:T(8,128)(2,1)} %broadcast_in_dim.33), calls=%async_computation | async-start | bytes 2097152 | tf_op jit(solution)/shard_map/all_to_all | solution.py:47
  78.0 48.8 %copy-start.4 = (bf16[8,5120]{1,0:T(8,128)(2,1)S(1)}, bf16[8,5120]{1,0:T(8,128)(2,1)}, u32[]{:S(2)}) copy-start(bf16[8,5120]{1,0:T(8,128)(2,1)} %param.18) | copy-start | bytes 245764
  103.4 23.2 %all-to-all-start.1 = ((bf16[16,8,320]{2,1,0:T(8,128)(2,1)}), bf16[16,8,320]{2,1,0:T(8,128)(2,1)S(1)}, u32[]{:S(2)}, u32[]{:S(2)}) async-start(bf16[16,8,320]{2,1,0:T(8,128)(2,1)} %bitcast.3), calls=%async_computation.1 | async-start | bytes 196608 | tf_op jit(solution)/shard_map/all_to_all | solution.py:54
  127.0 0.7 copy-start.3
  128.6 23.8 %all-to-all-start.2 = ((bf16[64,2,640]{2,1,0:T(2,128)(2,1)}), bf16[64,2,640]{2,1,0:T(2,128)(2,1)S(1)}, u32[]{:S(2)}, u32[]{:S(2)}) async-start(bf16[64,2,640]{2,1,0:T(2,128)(2,1)} %reshape.49), calls=%async_computation.2 | async-start | bytes 327680 | tf_op jit(solution)/shard_map/all_to_all | solution.py:82
  152.5 4.8 %collective-permute-start = (bf16[128,640]{1,0:T(8,128)(2,1)S(1)}, bf16[128,640]{1,0:T(8,128)(2,1)S(1)}, u32[]{:S(2)}, u32[]{:S(2)}) collective-permute-start(bf16[128,640]{1,0:T(8,128)(2,1)S(1)} %reshape.50), channel_id=1, source_target_pairs={{0,64},{64,128},{128,192},{192,256},{256,320},{320,384},{384,448},... | collective-permute-start | bytes 491528 | tf_op jit(solution)/shard_map/ppermute | solution.py:96
  157.2 4.7 %collective-permute-start.1 = (bf16[128,640]{1,0:T(8,128)(2,1)S(1)}, bf16[128,640]{1,0:T(8,128)(2,1)S(1)}, u32[]{:S(2)}, u32[]{:S(2)}) collective-permute-start(bf16[128,640]{1,0:T(8,128)(2,1)S(1)} %collective-permute-done), channel_id=1, source_target_pairs={{0,64},{64,128},{128,192},{192,256},{256,320},{320,384},{384,448},... | collective-permute-start | bytes 491528 | tf_op jit(solution)/shard_map/ppermute | solution.py:96
  157.8 4.7 %collective-permute-start.4 = (bf16[128,640]{1,0:T(8,128)(2,1)S(1)}, bf16[128,640]{1,0:T(8,128)(2,1)S(1)}, u32[]{:S(2)}, u32[]{:S(2)}) collective-permute-start(bf16[128,640]{1,0:T(8,128)(2,1)S(1)} %reshape.50), channel_id=1, source_target_pairs={{0,448},{64,0},{128,64},{192,128},{256,192},{320,256},{384,320},{4... | collective-permute-start | bytes 491528 | tf_op jit(solution)/shard_map/ppermute | solution.py:99
  162.0 0.7 copy-start.1
  162.0 4.8 %collective-permute-start.2 = (bf16[128,640]{1,0:T(8,128)(2,1)S(1)}, bf16[128,640]{1,0:T(8,128)(2,1)}, u32[]{:S(2)}, u32[]{:S(2)}) collective-permute-start(bf16[128,640]{1,0:T(8,128)(2,1)S(1)} %collective-permute-done.1), channel_id=1, source_target_pairs={{0,64},{64,128},{128,192},{192,256},{256,320},{320,384},{384,448},... | collective-permute-start | bytes 491528 | tf_op jit(solution)/shard_map/ppermute | solution.py:96
  162.7 16.7 %collective-permute-start.5 = (bf16[128,640]{1,0:T(8,128)(2,1)S(1)}, bf16[128,640]{1,0:T(8,128)(2,1)}, u32[]{:S(2)}, u32[]{:S(2)}) collective-permute-start(bf16[128,640]{1,0:T(8,128)(2,1)S(1)} %collective-permute-done.4), channel_id=1, source_target_pairs={{0,448},{64,0},{128,64},{192,128},{256,192},{320,256},{384,320},{4... | collective-permute-start | bytes 491528 | tf_op jit(solution)/shard_map/ppermute | solution.py:99
  166.8 12.7 %collective-permute-start.3 = (bf16[128,640]{1,0:T(8,128)(2,1)}, bf16[128,640]{1,0:T(8,128)(2,1)}, u32[]{:S(2)}, u32[]{:S(2)}) collective-permute-start(bf16[128,640]{1,0:T(8,128)(2,1)} %collective-permute-done.2), channel_id=1, source_target_pairs={{0,64},{64,128},{128,192},{192,256},{256,320},{320,384},{384,448},... | collective-permute-start | bytes 491528 | tf_op jit(solution)/shard_map/ppermute | solution.py:96
  168.4 40.9 %all-to-all-start.3 = ((bf16[96,8,640]{2,0,1:T(8,128)(2,1)}), bf16[96,8,640]{2,0,1:T(8,128)(2,1)S(1)}, u32[]{:S(2)}, u32[]{:S(2)}) async-start(bf16[96,8,640]{2,0,1:T(8,128)(2,1)} %copy.29), calls=%async_computation.3 | async-start | bytes 1966080 | tf_op jit(solution)/shard_map/all_to_all | solution.py:87
  179.4 15.1 %copy-start.2 = (bf16[128,640]{1,0:T(8,128)(2,1)S(1)}, bf16[128,640]{1,0:T(8,128)(2,1)}, u32[]{:S(2)}) copy-start(bf16[128,640]{1,0:T(8,128)(2,1)} %copy-done.1) | copy-start | bytes 491524
  179.4 13.2 %collective-permute-start.6 = (bf16[128,640]{1,0:T(8,128)(2,1)}, bf16[128,640]{1,0:T(8,128)(2,1)S(1)}, u32[]{:S(2)}, u32[]{:S(2)}) collective-permute-start(bf16[128,640]{1,0:T(8,128)(2,1)} %collective-permute-done.5), channel_id=1, source_target_pairs={{0,448},{64,0},{128,64},{192,128},{256,192},{320,256},{384,320},{4... | collective-permute-start | bytes 491528 | tf_op jit(solution)/shard_map/ppermute | solution.py:99
  195.6 19.3 %copy-start.6 = (f32[8,6]{1,0:T(8,128)S(1)}, f32[8,6]{1,0:T(8,128)}, u32[]{:S(2)}) copy-start(f32[8,6]{1,0:T(8,128)} %param.21) | copy-start | bytes 580
  210.3 24.4 %all-to-all-start.4 = ((bf16[64,2,640]{2,1,0:T(2,128)(2,1)}), bf16[64,2,640]{2,1,0:T(2,128)(2,1)S(1)}, u32[]{:S(2)}, u32[]{:S(2)}) async-start(bf16[64,2,640]{2,1,0:T(2,128)(2,1)} %reshape.52), calls=%async_computation.4 | async-start | bytes 327680 | tf_op jit(solution)/shard_map/all_to_all | solution.py:113
Sparse Core Ops, SparseCore 0:
  9.5 47.3 all-gather.2
